TPU v7x, 256 devices: a whole 4x4x8 slice. The times are simulated.
256 devices in a mesh: segment: 4 (over z_lo), expert: 64 (over x, y, z_hi, core).
Axes of the slice: x: 4, y: 4, z: 8 (z_hi: 2, z_lo: 4; z = z_hi * 4 + z_lo), core: 2. Of those that a mesh axis runs over, the one named last changes fastest.
Arguments:
- forward_input: bfloat16 [4, 512, 7168], P('segment', 'expert'), may hold values from -6 to 6
- forward_routes: int32 [4, 512, 8], P('segment', 'expert'), may hold values from 0 to 15, all different within a row; in each aligned block of 8 rows (0 to 7, 8 to 15, ..., all dimensions but the last counted through in order) at most 8 rows name the same one
- forward_gates: float32 [4, 512, 8], P('segment', 'expert'), may hold values from 0.05 to 0.8
- gate_matrix: bfloat16 [4, 64, 7168, 256], P('segment', 'expert'), may hold values from -0.0625 to 0.0625
- up_matrix: bfloat16 [4, 64, 7168, 256], P('segment', 'expert'), may hold values from -0.0625 to 0.0625
- down_matrix: bfloat16 [4, 64, 256, 7168], P('segment', 'expert'), may hold values from -0.1875 to 0.1875
Outputs:
- next_input: bfloat16 [4, 512, 7168], P('segment', 'expert')
Inputs may be any that keep to these rules, and one draw needn't show every extreme that they name: `forward_routes`: each token names 8 different experts. Among the 8 tokens of one index of expert, no expert is named by more than 8 of them, and in every draw some expert is named by exactly 8 tokens of some index.
All inputs are finite; a program needn't handle non-finite values.
Results may differ from a plain program's by a relative error of at most 0.0065.
Values may be sent and summed in bfloat16 or wider, within the bound.
No kernel may reach another device: no remote copies, remote signals or barrier semaphores. Data moves between devices by JAX's collectives and lax.ppermute only.
A program may use at most 128 MiB of HBM per device.

v0:
```python
import jax
import jax.numpy as jnp
from jax import lax
from jax.sharding import PartitionSpec as P

FH = 1024


def passed_along(value, axis, steps):
    count = lax.axis_size(axis)
    pairs = [(source, (source + steps) % count) for source in range(count)]
    return lax.ppermute(value, axis, pairs)


def local(forward_input, forward_routes, forward_gates, gate_matrix, up_matrix, down_matrix):
    devices = lax.axis_size("expert")
    hidden_slice = gate_matrix.shape[3]
    split = FH // hidden_slice
    groups = devices // split
    tokens = forward_input[0]
    me = lax.axis_index("expert")
    expert = me % groups
    rows = lax.all_gather(tokens, "expert", axis=0, tiled=True)
    routes = lax.all_gather(forward_routes[0], "expert", axis=0, tiled=True)
    gates = lax.all_gather(forward_gates[0], "expert", axis=0, tiled=True)
    weight = jnp.sum(jnp.where(routes == expert, gates, 0.0), axis=1)
    gate_act = jnp.dot(rows, gate_matrix[0, 0], preferred_element_type=jnp.float32)
    upper_act = jnp.dot(rows, up_matrix[0, 0], preferred_element_type=jnp.float32)
    hidden = (jax.nn.silu(gate_act) * upper_act).astype(jnp.bfloat16)
    partial = jnp.dot(hidden, down_matrix[0, 0], preferred_element_type=jnp.float32)
    partial = partial.astype(jnp.bfloat16).astype(jnp.float32)
    weighted = (weight[:, None] * partial).astype(jnp.bfloat16)
    mixed = lax.psum_scatter(weighted, "expert", scatter_dimension=0, tiled=True)
    layer_out = (tokens.astype(jnp.float32) + mixed.astype(jnp.float32)).astype(jnp.bfloat16)
    next_input = passed_along(layer_out, "segment", 1)
    return next_input[None]


def solution(mesh):
    in_specs = (
        P("segment", "expert", None),
        P("segment", "expert", None),
        P("segment", "expert", None),
        P("segment", "expert", None, None),
        P("segment", "expert", None, None),
        P("segment", "expert", None, None),
    )
    out_specs = P("segment", "expert", None)
    return jax.shard_map(local, mesh=mesh, in_specs=in_specs, out_specs=out_specs, check_vma=False)
```

profile of v0, /device:TPU:0, one launch (start us, length us, event | category | flops | bytes accessed | tf_op | source)
XLA Modules:
  0.0 718.2 jit_solution(15679720350931443463)
XLA Ops:
  6.5 0.0 all-gather.5.cloned.1.call-start
  6.5 0.7 all-gather.5.cloned.1.call-update
  7.3 0.0 reduce-scatter.2.cloned.1.call-start
  7.3 125.8 %all-gather = s32[1,512,8]{2,1,0:T(8,128)S(1)} all-gather(s32[1,8,8]{2,1,0:T(8,128)} %param.7), channel_id=2, replica_groups=mesh['segment'=4,'expert'=64] {'expert'}, dimensions={1}, use_global_device_ids=true | all-gather | bytes 16640 | tf_op jit(solution)/shard_map/all_gather | solution.py:24
  133.1 109.0 %all-gather.1 = f32[1,512,8]{2,1,0:T(8,128)S(1)} all-gather(f32[1,8,8]{2,1,0:T(8,128)} %param.8), channel_id=3, replica_groups=mesh['segment'=4,'expert'=64] {'expert'}, dimensions={1}, use_global_device_ids=true | all-gather | bytes 16640 | tf_op jit(solution)/shard_map/all_gather | solution.py:25
  242.1 0.1 select_reduce_fusion
  242.2 0.0 all-gather.5.cloned.1.call-done
  242.2 6.2 fusion.2
  248.4 15.9 %multiply_convert_fusion = bf16[512,7168]{1,0:T(8,128)(2,1)} fusion(f32[512]{0:T(512)S(1)} %select_reduce_fusion, bf16[1,1,256,7168]{3,2,1,0:T(8,128)(2,1)} %param.11, bf16[1,1,7168,256]{3,2,1,0:T(8,128)(2,1)} %param.10, bf16[1,512,7168]{2,1,0:T(8,128)(2,1)} %all-gather.5.cloned.1.call-done, f32[512,256]{1,0:T(8,128)S(1)} %fusion.2), kind=kOutput, calls=%fused_computation | convolution fusion | flops 3773562880 | bytes 22546432 | tf_op jit(solution)/shard_map/dot_general | solution.py:30
  264.4 0.0 copy-start
  264.4 0.0 reduce-scatter.2.cloned.1.call-update
  264.4 438.7 %reduce-scatter.2.cloned.1.call-done = bf16[8,7168]{1,0:T(8,128)(2,1)} async-done(((bf16[512,7168]{1,0:T(8,128)(2,1)}), bf16[8,7168]{1,0:T(8,128)(2,1)}) %reduce-scatter.2.cloned.1.call-update) | async-done | bytes 114704 | tf_op jit(solution)/shard_map/reduce_scatter | solution.py:33
  703.1 0.0 copy-done
  703.1 0.9 fusion.17
  704.0 0.1 collective-permute-start
  704.1 6.6 collective-permute-done
  710.7 0.6 copy.8
Async XLA Ops:
  6.5 235.7 %all-gather.5.cloned.1.call-start = ((), (), s32[]{:S(2)}) async-start(), calls=%async_computation.2 | async-start | bytes 7454720 | tf_op jit(solution)/shard_map/all_gather | solution.py:23
  7.3 695.9 %reduce-scatter.2.cloned.1.call-start = ((), (), s32[]{:S(2)}) async-start(), calls=%async_computation.1 | async-start | bytes 7454720 | tf_op jit(solution)/shard_map/reduce_scatter | solution.py:33
  264.4 438.7 %copy-start = (bf16[1,8,7168]{2,1,0:T(8,128)(2,1)S(1)}, bf16[1,8,7168]{2,1,0:T(8,128)(2,1)}, u32[]{:S(2)}) copy-start(bf16[1,8,7168]{2,1,0:T(8,128)(2,1)} %param.6) | copy-start | bytes 344068
  704.0 6.7 collective-permute-start
Sparse Core Ops, SparseCore 0:
  10.8 110.3 all-gather.4
  264.5 438.5 reduce-scatter.1
where the time goes:
time: 718 us
  waiting for transfers between devices  446 us (62%)
  blocking collectives  235 us (33%)
  matrix products  22.1 us (3%)
  between operations  13.4 us (2%)
    reduce_scatter x1, waiting for transfers between devices, local(): lax.psum_scatter(weighted, 'expert', scatter_dimension=0, tiled=True)  439 us
    all_gather x1, blocking collectives, local(): routes = lax.all_gather(forward_routes[0], 'expert', axis=0, tiled=True)  126 us
    all_gather x1, blocking collectives, local(): gates = lax.all_gather(forward_gates[0], 'expert', axis=0, tiled=True)  109 us
    dot_general x1, matrix products, local(): jnp.dot(hidden, down_matrix[0, 0], preferred_element_type=jnp.float32)  15.9 us
  transfers between devices with their start and end apart: 3, of which 2 were waited for; matrix products, arithmetic and copies ran while one was open for 0% of the time, Pallas kernels for 0%

commit v1 on v0

--- a/solution.py
+++ b/solution.py
@@ -4,6 +4,15 @@
 from jax.sharding import PartitionSpec as P
 
 FH = 1024
+attach_stocks = lambda on_dim, target: jnp.concatenate(
+    lax.all_to_all(
+        jnp.stack([target for _ in range(lax.axis_size("expert"))]),
+        concat_axis=0,
+        axis_name="expert",
+        split_axis=0,
+    ),
+    on_dim,
+)
 
 
 def passed_along(value, axis, steps):
@@ -22,7 +31,7 @@
     expert = me % groups
     rows = lax.all_gather(tokens, "expert", axis=0, tiled=True)
     routes = lax.all_gather(forward_routes[0], "expert", axis=0, tiled=True)
-    gates = lax.all_gather(forward_gates[0], "expert", axis=0, tiled=True)
+    gates = attach_stocks(0, forward_gates[0])
     weight = jnp.sum(jnp.where(routes == expert, gates, 0.0), axis=1)
     gate_act = jnp.dot(rows, gate_matrix[0, 0], preferred_element_type=jnp.float32)
     upper_act = jnp.dot(rows, up_matrix[0, 0], preferred_element_type=jnp.float32)

time: 718 us -> 615 us (0.86)
  blocking collectives: 235 us -> 122 us
  starting transfers between devices: 0.12 us -> 14 us
    all_gather x1 -> x0, blocking collectives: 109 us -> none  [local(): gates = lax.all_gather(forward_gates[0], 'expert', axis=0, tiled=True)]
    all_to_all x0 -> x1, starting transfers between devices: none -> 12.9 us  [lax.all_to_all(jnp.stack([target for _ in range(lax.axis_size('expert'))]...]
  transfers between devices with their start and end apart: 3 -> 4, of which waited for: 2 -> 2; matrix products, arithmetic and copies ran while one was open for 0% -> 0% of each run, Pallas kernels for 0% -> 0%
where the time goes in v1:
time: 615 us
  waiting for transfers between devices  440 us (72%)
  blocking collectives  122 us (20%)
  matrix products  22.2 us (4%)
  starting transfers between devices  14 us (2%)
  between operations  13.4 us (2%)
    reduce_scatter x1, waiting for transfers between devices, local(): lax.psum_scatter(weighted, 'expert', scatter_dimension=0, tiled=True)  433 us
    all_gather x1, blocking collectives, local(): routes = lax.all_gather(forward_routes[0], 'expert', axis=0, tiled=True)  122 us
    dot_general x1, matrix products, local(): jnp.dot(hidden, down_matrix[0, 0], preferred_element_type=jnp.float32)  16 us
    all_to_all x1, starting transfers between devices, lax.all_to_all(jnp.stack([target for _ in range(lax.axis_size('expert'))]...  12.9 us
  transfers between devices with their start and end apart: 4, of which 2 were waited for; matrix products, arithmetic and copies ran while one was open for 0% of the time, Pallas kernels for 0%

profile of v1, /device:TPU:0, one launch (start us, length us, event | category | flops | bytes accessed | tf_op | source)
XLA Modules:
  0.0 614.6 jit_solution(10083953702663133053)
XLA Ops:
  6.5 0.0 all-gather.4.cloned.1.call-start
  6.5 0.7 all-gather.4.cloned.1.call-update
  7.3 1.4 stack.3
  8.7 12.9 %all-to-all-start = ((f32[64,8,8]{2,1,0:T(8,128)}), f32[64,8,8]{2,1,0:T(8,128)S(1)}, u32[]{:S(2)}, u32[]{:S(2)}) async-start(f32[64,8,8]{2,1,0:T(8,128)} %stack.3), calls=%async_computation | async-start | bytes 524288 | tf_op jit(solution)/shard_map/all_to_all | solution.py:8
  21.5 0.0 reduce-scatter.2.cloned.1.call-start
  21.6 122.2 %all-gather = s32[1,512,8]{2,1,0:T(8,128)S(1)} all-gather(s32[1,8,8]{2,1,0:T(8,128)} %param.7), channel_id=2, replica_groups=mesh['segment'=4,'expert'=64] {'expert'}, dimensions={1}, use_global_device_ids=true | all-gather | bytes 16640 | tf_op jit(solution)/shard_map/all_gather | solution.py:33
  143.8 0.0 all-to-all-done
  143.8 0.2 fusion.17
  144.0 0.0 all-gather.4.cloned.1.call-done
  144.0 6.2 %fusion.2 = f32[512,256]{1,0:T(8,128)S(1)} fusion(bf16[1,512,7168]{2,1,0:T(8,128)(2,1)} %all-gather.4.cloned.1.call-done, bf16[1,1,7168,256]{3,2,1,0:T(8,128)(2,1)} %param.9), kind=kOutput, calls=%fused_computation.4 | convolution fusion | flops 1879048192 | bytes 11534336 | tf_op jit(solution)/shard_map/dot_general | solution.py:36
  150.2 16.0 %multiply_convert_fusion = bf16[512,7168]{1,0:T(8,128)(2,1)} fusion(f32[512]{0:T(512)S(1)} %fusion.17, bf16[1,1,256,7168]{3,2,1,0:T(8,128)(2,1)} %param.11, bf16[1,1,7168,256]{3,2,1,0:T(8,128)(2,1)} %param.10, bf16[1,512,7168]{2,1,0:T(8,128)(2,1)} %all-gather.4.cloned.1.call-done, f32[512,256]{1,0:T(8,128)S(1)} %fusion.2), kind=kOutput, calls=%fused_computation | convolution fusion | flops 3773562880 | bytes 22546432 | tf_op jit(solution)/shard_map/dot_general | solution.py:39
  166.2 0.0 copy-start
  166.2 0.0 reduce-scatter.2.cloned.1.call-update
  166.2 433.3 %reduce-scatter.2.cloned.1.call-done = bf16[8,7168]{1,0:T(8,128)(2,1)} async-done(((bf16[512,7168]{1,0:T(8,128)(2,1)}), bf16[8,7168]{1,0:T(8,128)(2,1)}) %reduce-scatter.2.cloned.1.call-update) | async-done | bytes 114704 | tf_op jit(solution)/shard_map/reduce_scatter | solution.py:42
  599.6 0.0 copy-done
  599.6 0.9 fusion.18
  600.5 1.1 collective-permute-start
  601.6 5.6 collective-permute-done
  607.2 0.6 copy.8
Async XLA Ops:
  6.5 137.5 %all-gather.4.cloned.1.call-start = ((), (), s32[]{:S(2)}) async-start(), calls=%async_computation.3 | async-start | bytes 7454720 | tf_op jit(solution)/shard_map/all_gather | solution.py:32
  8.7 135.1 %all-to-all-start = ((f32[64,8,8]{2,1,0:T(8,128)}), f32[64,8,8]{2,1,0:T(8,128)S(1)}, u32[]{:S(2)}, u32[]{:S(2)}) async-start(f32[64,8,8]{2,1,0:T(8,128)} %stack.3), calls=%async_computation | async-start | bytes 524288 | tf_op jit(solution)/shard_map/all_to_all | solution.py:8
  21.5 578.0 %reduce-scatter.2.cloned.1.call-start = ((), (), s32[]{:S(2)}) async-start(), calls=%async_computation.2 | async-start | bytes 7454720 | tf_op jit(solution)/shard_map/reduce_scatter | solution.py:42
  166.2 433.4 %copy-start = (bf16[1,8,7168]{2,1,0:T(8,128)(2,1)S(1)}, bf16[1,8,7168]{2,1,0:T(8,128)(2,1)}, u32[]{:S(2)}) copy-start(bf16[1,8,7168]{2,1,0:T(8,128)(2,1)} %param.6) | copy-start | bytes 344068
  600.5 6.7 %collective-permute-start = (bf16[8,7168]{1,0:T(8,128)(2,1)S(1)}, bf16[8,7168]{1,0:T(8,128)(2,1)S(1)}, u32[]{:S(2)}, u32[]{:S(2)}) collective-permute-start(bf16[8,7168]{1,0:T(8,128)(2,1)S(1)} %fusion.18), channel_id=1, source_target_pairs={{0,64},{64,128},{128,192},{192,0},{1,65},{65,129},{129,193},{193,1... | collective-permute-start | bytes 344072 | tf_op jit(solution)/shard_map/ppermute | solution.py:21
Sparse Core Ops, SparseCore 0:
  10.8 111.5 all-gather.3
  166.3 433.1 reduce-scatter.1
